TPU v7x, 32 devices: a whole 2x2x4 slice. The times are simulated.
32 devices in a mesh: groups: 2 (over x), heads: 4 (over y, core), seq: 4 (over z).
Axes of the slice: x: 2, y: 2, z: 4, core: 2. Of those that a mesh axis runs over, the one named last changes fastest.
Arguments:
- lin_query: bfloat16 [4096, 4096], P(('groups', 'seq'), 'heads'), parts along dimension 0, may hold values from -6 to 6
- lin_key: bfloat16 [4096, 4096], P(('groups', 'seq'), 'heads'), parts along dimension 0, may hold values from -6 to 6
- lin_value: bfloat16 [4096, 4096], P(('groups', 'seq'), 'heads'), parts along dimension 0, may hold values from -6 to 6
- log_decay: float32 [4096, 32], P(('groups', 'seq'), 'heads'), parts along dimension 0, may hold values from -1 to 0
- stream: bfloat16 [4096, 6144], P(('groups', 'seq'), 'heads'), parts along dimension 0, may hold values from -400 to 400
- out_weight: bfloat16 [4096, 6144], P('heads', 'seq'), may hold values from -0.125 to 0.125
- norm_gain: bfloat16 [6144], P('heads'), may hold values from 0.5 to 1.5
- query_weight: bfloat16 [6144, 4096], P('seq', 'heads'), may hold values from -12 to 12
- kv_weight: bfloat16 [4, 6144, 256], P(None, 'seq'), may hold values from -1 to 1
Outputs:
- stream_next: bfloat16 [4096, 6144], P(('groups', 'seq'), 'heads'), parts along dimension 0
- attended: bfloat16 [4096, 4096], P(('groups', 'seq'), 'heads'), parts along dimension 0
There are 2 independent parts, one for each index of `groups`. A program takes and returns all parts, laid end to end along the dimension named above; an argument that names none is the same for every part. Nothing has to cross between parts.
All inputs are finite; a program needn't handle non-finite values.
Results may differ from a plain program's by a relative error of at most 0.019.
Values may be sent and summed in bfloat16 or wider, within the bound.
No kernel may reach another device: no remote copies, remote signals or barrier semaphores. Data moves between devices by JAX's collectives and lax.ppermute only.
A program may use at most 128 MiB of HBM per device.

v0:
```python
import jax
import jax.numpy as jnp
from jax import lax
from jax.sharding import PartitionSpec as P

D = 6144
QUERY_HEADS = 32
KVH = 4
DH = 128
BLOCK = 256


def from_behind(value, axis, steps):
    count = lax.axis_size(axis)
    leading, last = (max(0, -steps), min(count, count - steps))
    return lax.ppermute(value, axis, [(source, source + steps) for source in range(leading, last)])


def lightning_block(kv_state, block_inputs):
    query_blk, key_blk, value_blk, decay_blk = block_inputs
    block_len = query_blk.shape[0]
    local_cum = jnp.cumsum(decay_blk, axis=0)
    causal_mask = (jnp.arange(block_len)[:, None] >= jnp.arange(block_len)[None, :])[:, :, None]
    decay_diff = local_cum[:, None, :] - local_cum[None, :, :]
    decays = jnp.where(causal_mask, jnp.exp(jnp.where(causal_mask, decay_diff, 0.0)), 0.0)
    scores = jnp.einsum("thd,shd->hts", query_blk, key_blk, preferred_element_type=jnp.float32)
    weights = (scores * jnp.transpose(decays, (2, 0, 1))).astype(jnp.bfloat16)
    intra_out = jnp.einsum("hts,shd->thd", weights, value_blk, preferred_element_type=jnp.float32)
    query_f = query_blk.astype(jnp.float32)
    inter_out = jnp.einsum(
        "thd,hde->the",
        query_f * jnp.exp(local_cum)[:, :, None],
        kv_state,
        precision=lax.Precision.HIGHEST,
    )
    tail_decay = jnp.exp(local_cum[-1][None, :] - local_cum)
    key_f = key_blk.astype(jnp.float32) * tail_decay[:, :, None]
    kv_state = jnp.exp(local_cum[-1])[:, None, None] * kv_state + jnp.einsum(
        "shd,she->hde", key_f, value_blk.astype(jnp.float32), precision=lax.Precision.HIGHEST
    )
    return (kv_state, intra_out + inter_out)


def shards(
    lin_query, lin_key, lin_value, log_decay, stream, out_weight, norm_gain, query_weight, kv_weight
):
    tok_rows = lin_query.shape[0]
    heads_here = log_decay.shape[1]
    head_width = heads_here * DH
    nblocks = tok_rows // BLOCK
    block_shape = (nblocks, BLOCK, heads_here, DH)
    inputs = (
        lin_query.reshape(block_shape),
        lin_key.reshape(block_shape),
        lin_value.reshape(block_shape),
        log_decay.reshape(nblocks, BLOCK, heads_here),
    )
    start_state = jnp.zeros((heads_here, DH, DH), jnp.float32)
    local_state, local_out = lax.scan(lightning_block, start_state, inputs)
    local_out = local_out.reshape(tok_rows, heads_here, DH)
    decay_total = jnp.sum(log_decay, axis=0)
    totals, states = (
        lax.all_gather(decay_total[None].astype(jnp.bfloat16), "seq", axis=0, tiled=True).astype(
            jnp.float32
        ),
        lax.all_gather(local_state[None].astype(jnp.bfloat16), "seq", axis=0, tiled=True).astype(
            jnp.float32
        ),
    )
    position = lax.axis_index("seq")
    device_order = jnp.arange(totals.shape[0])
    earlier = (device_order < position)[:, None]
    before = jnp.sum(jnp.where(earlier, totals, 0.0), axis=0)
    inclusive = jnp.cumsum(totals, axis=0)
    factors = jnp.where(earlier, jnp.exp(jnp.where(earlier, before[None, :] - inclusive, 0.0)), 0.0)
    incoming = jnp.einsum("jh,jhde->hde", factors, states, precision=lax.Precision.HIGHEST)
    running = jnp.cumsum(log_decay, axis=0)
    query_f = (
        lin_query.reshape(tok_rows, heads_here, DH).astype(jnp.float32)
        * jnp.exp(running)[:, :, None]
    )
    carried = jnp.einsum("thd,hde->the", query_f, incoming, precision=lax.Precision.HIGHEST)
    lin_raw = local_out + carried
    lin_out = (
        (lin_raw * lax.rsqrt(jnp.mean(lin_raw * lin_raw, axis=-1, keepdims=True) + 1e-06))
        .astype(jnp.bfloat16)
        .reshape(tok_rows, head_width)
    )
    branch = jnp.dot(
        lin_out,
        lax.all_gather(out_weight, "seq", axis=1, tiled=True),
        preferred_element_type=jnp.float32,
    )
    kv_group = lax.axis_index("heads") * heads_here // (QUERY_HEADS // KVH)
    kv_mine = lax.dynamic_index_in_dim(kv_weight, kv_group, 0, keepdims=False)
    query_rows, kv_rows = (
        lax.all_gather(query_weight, "seq", axis=0, tiled=True),
        lax.all_gather(kv_mine, "seq", axis=0, tiled=True),
    )
    projection = jnp.concatenate([query_rows, kv_rows], axis=1)
    own_sum = lax.psum_scatter(
        branch.astype(jnp.bfloat16), "heads", scatter_dimension=1, tiled=True
    ).astype(jnp.float32)
    mixed_sum = stream.astype(jnp.float32) + own_sum
    stream_next = mixed_sum.astype(jnp.bfloat16)
    total_sq = lax.psum(jnp.sum(mixed_sum * mixed_sum, axis=1), "heads")
    normed = (
        mixed_sum
        * lax.rsqrt(total_sq / D + 1e-05)[:, None]
        * norm_gain.astype(jnp.float32)[None, :]
    ).astype(jnp.bfloat16)
    projected = jnp.dot(
        lax.all_gather(normed, "heads", axis=1, tiled=True),
        projection,
        preferred_element_type=jnp.float32,
    )
    projected = projected.astype(jnp.bfloat16)
    queries = projected[:, :head_width].reshape(tok_rows, heads_here, DH)
    keys_values = projected[:, head_width:]
    position = lax.axis_index("seq")
    query_pos = position * tok_rows + jnp.arange(tok_rows)
    score_scale = float(DH) ** (-0.5)

    def attend(state_in, kv_block, key_start):
        old_max, row_total, weighted = state_in
        key_count = kv_block.shape[0]
        key_part = kv_block[:, :DH]
        value_part = kv_block[:, DH:]
        scores = (
            jnp.einsum("thd,sd->hts", queries, key_part, preferred_element_type=jnp.float32)
            * score_scale
        )
        key_pos = key_start + jnp.arange(key_count)
        allowed = ((key_pos[None, :] <= query_pos[:, None]) & (key_pos[None, :] >= 0))[None, :, :]
        scores = jnp.where(allowed, scores, -1e30)
        new_max = jnp.maximum(old_max, jnp.max(scores, axis=-1))
        expos = jnp.where(allowed, jnp.exp(scores - new_max[:, :, None]), 0.0)
        rescale = jnp.exp(old_max - new_max)
        row_total = row_total * rescale + jnp.sum(expos, axis=-1)
        prob_bf16 = expos.astype(jnp.bfloat16)
        weighted = weighted * rescale[:, :, None] + jnp.einsum(
            "hts,sd->htd", prob_bf16, value_part, preferred_element_type=jnp.float32
        )
        return (new_max, row_total, weighted)

    initial = (
        jnp.full((heads_here, tok_rows), -1e30, jnp.float32),
        jnp.zeros((heads_here, tok_rows), jnp.float32),
        jnp.zeros((heads_here, tok_rows, DH), jnp.float32),
    )
    first_state = attend(initial, keys_values, position * tok_rows)
    seq_count = lax.axis_size("seq")

    def cycle_turn(turn_index, loop_state):
        moving, inner_state = loop_state
        moving = from_behind(moving, "seq", 1)
        source = position - turn_index
        return (moving, attend(inner_state, moving, source * tok_rows))

    _, final_state = lax.fori_loop(1, seq_count, cycle_turn, (keys_values, first_state))
    _, row_total, weighted = final_state
    attended = (
        jnp.transpose(weighted / row_total[:, :, None], (1, 0, 2))
        .reshape(tok_rows, head_width)
        .astype(jnp.bfloat16)
    )
    return (stream_next, attended)


def solution(mesh):
    return jax.shard_map(
        shards,
        mesh=mesh,
        in_specs=(
            P(("groups", "seq"), "heads"),
            P(("groups", "seq"), "heads"),
            P(("groups", "seq"), "heads"),
            P(("groups", "seq"), "heads"),
            P(("groups", "seq"), "heads"),
            P("heads", "seq"),
            P("heads"),
            P("seq", "heads"),
            P(None, "seq", None),
        ),
        out_specs=(P(("groups", "seq"), "heads"), P(("groups", "seq"), "heads")),
        check_vma=False,
    )
```

profile of v0, /device:TPU:0, one launch (start us, length us, event | category | flops | bytes accessed | tf_op | source)
XLA Modules:
  0.0 828.3 jit_solution(3079648835785859866)
XLA Ops:
  7.3 2.6 copy.92
  9.9 2.5 copy.93
  13.6 79.9 %while.34 = (s32[]{:T(128)}, f32[8,128,128]{2,1,0:T(8,128)}, f32[2,256,8,128]{1,0,3,2:T(2,128)}, f32[2,256,8]{1,2,0:T(8,128)S(1)}, bf16[2,256,8,128]{3,2,1,0:T(8...) while((s32[]{:T(128)}, f32[8,128,128]{2,1,0:T(8,128)}, ...), condition=%wide.region_3.4_spmd.clone, body=%wide.region_0.3_spmd.clone.sunk | while | flops 1078530048 | bytes 19645352 | solution.py:59
  14.5 2.3 constant_dynamic-slice_fusion.7
  16.8 3.5 convolution_bitcast_fusion.2
  21.6 2.2 convolution_add_fusion.2
  23.9 3.8 fusion.84
  27.7 3.3 copy.136
  31.0 22.0 %dynamic_update_slice.6 = f32[2,256,8,128]{1,0,3,2:T(2,128)} dynamic-update-slice(f32[2,256,8,128]{1,0,3,2:T(2,128)} %get-tuple-element.452, f32[1,256,8,128]{1,0,3,2:T(1,128)} %copy.136, s32[]{:T(128)S(6)} %copy.141, s32[]{:T(128)} %constant.109.clone.1..sunk, s32[]{:T(128)} %constant.109.clone.1..sunk, s32[]{:T(128)} %constant.109.clone.1..sunk) | dynamic-update-slice | bytes 2097156 | tf_op jit(solution)/shard_map/while/body/jit(dynamic_update_index_in_dim)/dynamic_update_slice | solution.py:59
  53.8 2.3 constant_dynamic-slice_fusion.7
  56.0 3.7 convolution_bitcast_fusion.2
  61.1 3.4 convolution_add_fusion.2
  64.5 3.8 fusion.84
  68.3 3.3 copy.136
  71.6 22.0 %dynamic_update_slice.6 = f32[2,256,8,128]{1,0,3,2:T(2,128)} dynamic-update-slice(f32[2,256,8,128]{1,0,3,2:T(2,128)} %get-tuple-element.452, f32[1,256,8,128]{1,0,3,2:T(1,128)} %copy.136, s32[]{:T(128)S(6)} %copy.141, s32[]{:T(128)} %constant.109.clone.1..sunk, s32[]{:T(128)} %constant.109.clone.1..sunk, s32[]{:T(128)} %constant.109.clone.1..sunk) | dynamic-update-slice | bytes 2097156 | tf_op jit(solution)/shard_map/while/body/jit(dynamic_update_index_in_dim)/dynamic_update_slice | solution.py:59
  93.5 1.8 convert_element_type.87
  96.3 3.9 reshape.219
  101.7 14.2 %all-reduce = bf16[32]{0:T(256)(128)(2,1)S(1)} all-reduce(bf16[32]{0:T(256)(128)(2,1)S(1)} %dynamic-update-slice), channel_id=2, replica_groups=mesh['groups'=2,'heads'=4,'seq'=4] {'seq'}, use_global_device_ids=true, to_apply=%add | all-reduce | flops 32 | bytes 128
  117.6 8.8 %all-gather.15.cloned.1.call-done = bf16[32,128,128]{2,1,0:T(8,128)(2,1)} async-done(((bf16[8,128,128]{2,1,0:T(8,128)(2,1)}), bf16[32,128,128]{2,1,0:T(8,128)(2,1)}) %all-gather.15.cloned.1.call-update) | async-done | bytes 1048592 | tf_op jit(solution)/shard_map/all_gather | solution.py:66
  126.4 1.6 multiply_reduce_fusion.1
  127.9 4.7 multiply_reduce_fusion.2
  133.9 211.7 %all-gather.9.cloned.1.call-done = bf16[1024,6144]{1,0:T(8,128)(2,1)} async-done(((bf16[1024,1536]{1,0:T(8,128)(2,1)}), bf16[1024,6144]{1,0:T(8,128)(2,1)}) %all-gather.9.cloned.1.call-update) | async-done | bytes 12582928 | tf_op jit(solution)/shard_map/all_gather | solution.py:91
  345.6 11.8 %convolution_convert_fusion = bf16[512,6144]{1,0:T(8,128)(2,1)} fusion(bf16[512,1024]{0,1:T(8,128)(2,1)} %bitcast.181, bf16[1024,6144]{1,0:T(8,128)(2,1)} %all-gather.9.cloned.1.call-done), kind=kOutput, calls=%fused_computation.60 | convolution fusion | flops 6445596672 | bytes 19922944 | tf_op jit(solution)/shard_map/dot_general | solution.py:89
  359.1 54.5 %reduce-scatter.2.cloned.1.call-done = bf16[512,1536]{1,0:T(8,128)(2,1)} async-done(((bf16[512,6144]{1,0:T(8,128)(2,1)}), bf16[512,1536]{1,0:T(8,128)(2,1)}) %reduce-scatter.2.cloned.1.call-update) | async-done | bytes 1572880 | tf_op jit(solution)/shard_map/reduce_scatter | solution.py:101
  413.7 2.1 multiply_reduce_fusion
  415.8 6.0 psum.7
  421.8 2.3 multiply_convert_fusion.1
  424.4 54.7 %all-gather.17.cloned.1.call-done = bf16[1,6144,256]{2,1,0:T(8,128)(2,1)} async-done(((bf16[1,1536,256]{2,1,0:T(8,128)(2,1)}), bf16[1,6144,256]{2,1,0:T(8,128)(2,1)}) %all-gather.17.cloned.1.call-update) | async-done | bytes 3145744 | tf_op jit(solution)/shard_map/all_gather | solution.py:98
  479.1 218.3 %all-gather.13.cloned.1.call-done = bf16[6144,1024]{1,0:T(8,128)(2,1)} async-done(((bf16[1536,1024]{1,0:T(8,128)(2,1)}), bf16[6144,1024]{1,0:T(8,128)(2,1)}) %all-gather.13.cloned.1.call-update) | async-done | bytes 12582928 | tf_op jit(solution)/shard_map/all_gather | solution.py:97
  697.4 46.0 %all-gather.11.cloned.1.call-done = bf16[512,6144]{1,0:T(8,128)(2,1)} async-done(((bf16[512,1536]{1,0:T(8,128)(2,1)}), bf16[512,6144]{1,0:T(8,128)(2,1)}) %all-gather.11.cloned.1.call-update) | async-done | bytes 6291472 | tf_op jit(solution)/shard_map/all_gather | solution.py:113
  743.4 15.6 %fusion.43 = bf16[512,1280]{1,0:T(8,128)(2,1)S(1)} fusion(bf16[512,6144]{1,0:T(8,128)(2,1)} %all-gather.11.cloned.1.call-done, bf16[6144,256]{1,0:T(8,128)(2,1)} %bitcast.188, bf16[6144,1024]{1,0:T(8,128)(2,1)} %all-gather.13.cloned.1.call-done), kind=kOutput, calls=%fused_computation.71 | convolution fusion | flops 8085176320 | bytes 23330816 | tf_op jit(solution)/shard_map/dot_general | solution.py:112
  759.2 1.5 fusion.37
  760.7 2.0 fusion.39
  762.8 3.9 fusion.49
  766.7 51.9 %while.33 = (s32[]{:T(128)}, bf16[512,256]{1,0:T(8,128)(2,1)S(1)}, f32[8,512]{1,0:T(8,128)S(1)}, f32[8,512]{1,0:T(8,128)S(1)}, f32[8,512,128]{2,1,0:T(8,128)}, /...) while((s32[]{:T(128)}, bf16[512,256]{1,0:T(8,128)(2,1)S(1)}, ...), condition=%wide.region_18.19_spmd.clone, body=%wide.region_15.18_spmd.clone.sunk | while | flops 1102587904 | bytes 50341096 | solution.py:160
  766.7 3.4 collective-permute-start
  770.4 5.7 collective-permute-done
  777.6 2.0 fusion.79
  779.7 3.1 multiply_add_fusion.5
  784.2 4.4 collective-permute-start
  788.9 4.8 collective-permute-done
  795.3 2.0 fusion.79
  797.4 3.1 multiply_add_fusion.5
  801.8 4.4 collective-permute-start
  806.5 3.9 collective-permute-done
  812.0 2.0 fusion.79
  814.1 3.1 multiply_add_fusion.5
  818.6 2.9 copy_bitcast_fusion.11
  (125 shorter events, 22.3 us)
Async XLA Ops:
  7.2 350.3 %copy-start = (bf16[4,1536,256]{2,1,0:T(8,128)(2,1)S(1)}, bf16[4,1536,256]{2,1,0:T(8,128)(2,1)}, u32[]{:S(2)}) copy-start(bf16[4,1536,256]{2,1,0:T(8,128)(2,1)} %param.21) | copy-start | bytes 9437188
  7.2 119.2 %all-gather.15.cloned.1.call-start = ((), (), s32[]{:S(2)}) async-start(), calls=%async_computation.5 | async-start | bytes 1310720 | tf_op jit(solution)/shard_map/all_gather | solution.py:66
  7.2 5.1 copy-start.6
  7.3 6.4 copy-start.9
  16.7 4.9 copy-start.2
  21.6 2.2 copy-start.3
  56.0 5.0 copy-start.2
  61.0 3.4 copy-start.3
  95.3 4.9 copy-start.11
  95.4 250.2 %all-gather.9.cloned.1.call-start = ((), (), s32[]{:S(2)}) async-start(), calls=%async_computation.1 | async-start | bytes 15728640 | tf_op jit(solution)/shard_map/all_gather | solution.py:91
  96.1 317.6 %reduce-scatter.2.cloned.1.call-start = ((), (), s32[]{:S(2)}) async-start(), calls=%async_computation.2 | async-start | bytes 7864320 | tf_op jit(solution)/shard_map/reduce_scatter | solution.py:101
  357.4 1.7 copy-start.10
  357.4 121.7 %all-gather.17.cloned.1.call-start = ((), (), s32[]{:S(2)}) async-start(), calls=%async_computation.6 | async-start | bytes 3932160 | tf_op jit(solution)/shard_map/all_gather | solution.py:98
  358.4 55.2 %copy-start.4 = (bf16[512,1536]{1,0:T(8,128)(2,1)S(1)}, bf16[512,1536]{1,0:T(8,128)(2,1)}, u32[]{:S(2)}) copy-start(bf16[512,1536]{1,0:T(8,128)(2,1)} %param.17) | copy-start | bytes 4718596
  358.5 338.9 %all-gather.13.cloned.1.call-start = ((), (), s32[]{:S(2)}) async-start(), calls=%async_computation.4 | async-start | bytes 15728640 | tf_op jit(solution)/shard_map/all_gather | solution.py:97
  359.1 384.3 %all-gather.11.cloned.1.call-start = ((), (), s32[]{:S(2)}) async-start(), calls=%async_computation.3 | async-start | bytes 7864320 | tf_op jit(solution)/shard_map/all_gather | solution.py:113
  413.7 8.1 copy-start.5
  766.7 9.3 %collective-permute-start = (bf16[512,256]{1,0:T(8,128)(2,1)S(1)}, bf16[512,256]{1,0:T(8,128)(2,1)S(1)}, u32[]{:S(2)}, u32[]{:S(2)}) collective-permute-start(bf16[512,256]{1,0:T(8,128)(2,1)S(1)} %get-tuple-element.481), channel_id=1, source_target_pairs={{0,1},{1,2},{2,3},{4,5},{5,6},{6,7},{8,9},{9,10},{10,11},{12,13},{... | collective-permute-start | bytes 786440 | tf_op jit(solution)/shard_map/while/body/eval_jaxpr/ppermute | solution.py:16
  777.6 2.1 copy-start.7
  782.9 1.4 copy-start.8
  784.2 9.5 %collective-permute-start = (bf16[512,256]{1,0:T(8,128)(2,1)S(1)}, bf16[512,256]{1,0:T(8,128)(2,1)S(1)}, u32[]{:S(2)}, u32[]{:S(2)}) collective-permute-start(bf16[512,256]{1,0:T(8,128)(2,1)S(1)} %get-tuple-element.481), channel_id=1, source_target_pairs={{0,1},{1,2},{2,3},{4,5},{5,6},{6,7},{8,9},{9,10},{10,11},{12,13},{... | collective-permute-start | bytes 786440 | tf_op jit(solution)/shard_map/while/body/eval_jaxpr/ppermute | solution.py:16
  795.2 2.1 copy-start.7
  800.5 1.4 copy-start.8
  801.8 8.6 %collective-permute-start = (bf16[512,256]{1,0:T(8,128)(2,1)S(1)}, bf16[512,256]{1,0:T(8,128)(2,1)S(1)}, u32[]{:S(2)}, u32[]{:S(2)}) collective-permute-start(bf16[512,256]{1,0:T(8,128)(2,1)S(1)} %get-tuple-element.481), channel_id=1, source_target_pairs={{0,1},{1,2},{2,3},{4,5},{5,6},{6,7},{8,9},{9,10},{10,11},{12,13},{... | collective-permute-start | bytes 786440 | tf_op jit(solution)/shard_map/while/body/eval_jaxpr/ppermute | solution.py:16
  812.0 2.1 copy-start.7
  817.2 1.4 copy-start.8
  818.6 2.9 copy-start.1
Sparse Core Ops, SparseCore 0:
  95.5 30.8 all-gather.14
  127.9 217.6 all-gather.8
  357.5 56.0 reduce-scatter.1
  415.7 63.4 all-gather.16
  480.5 216.8 all-gather.12
  698.8 44.5 all-gather.10
where the time goes:
time: 832 us; the launch traced here: 828 us
  waiting for transfers between devices  610 us (73%)
  local copies, waits for them, and re-layouts  74.6 us (9%)
  matrix products  71.7 us (9%)
  other arithmetic  24.5 us (3%)
  blocking collectives  20.1 us (2%)
  between operations  15 us (2%)
  starting transfers between devices  12.4 us (1%)
    all_gather x1, waiting for transfers between devices, shards(): lax.all_gather(query_weight, 'seq', axis=0, tiled=True)  218 us
    all_gather x1, waiting for transfers between devices, shards(): lax.all_gather(out_weight, 'seq', axis=1, tiled=True)  212 us
    all_gather x1, waiting for transfers between devices, shards(): lax.all_gather(kv_mine, 'seq', axis=0, tiled=True)  54.7 us
    reduce_scatter x1, waiting for transfers between devices, shards(): lax.psum_scatter(branch.astype(jnp.bfloat16), 'heads', scatter_dimension=...  54.5 us
    dynamic_update_slice x4, local copies, waits for them, and re-layouts, shards(): local_state, local_out = lax.scan(lightning_block, start_state, inputs)  50.5 us
    all_gather x1, waiting for transfers between devices, shards(): lax.all_gather(normed, 'heads', axis=1, tiled=True)  46 us
  transfers between devices with their start and end apart: 9, of which 9 were waited for; matrix products, arithmetic and copies ran while one was open for 2% of the time, Pallas kernels for 0%

commit v1 on v0

--- a/solution.py
+++ b/solution.py
@@ -8,6 +8,18 @@
 KVH = 4
 DH = 128
 BLOCK = 256
+
+
+def doubled_up(x, axis, dim):
+    ways, here, lap = (lax.axis_size(axis), lax.axis_index(axis), x.shape[dim])
+    line, have = (x, 1)
+    while have < ways:
+        line = jnp.concatenate(
+            [line, lax.ppermute(line, axis, [(d, (d - have) % ways) for d in range(ways)])],
+            axis=dim,
+        )
+        have = 2 * have
+    return jnp.roll(line, here * lap, axis=dim)
 
 
 def from_behind(value, axis, steps):
@@ -110,9 +122,7 @@
         * norm_gain.astype(jnp.float32)[None, :]
     ).astype(jnp.bfloat16)
     projected = jnp.dot(
-        lax.all_gather(normed, "heads", axis=1, tiled=True),
-        projection,
-        preferred_element_type=jnp.float32,
+        doubled_up(normed, "heads", 1), projection, preferred_element_type=jnp.float32
     )
     projected = projected.astype(jnp.bfloat16)
     queries = projected[:, :head_width].reshape(tok_rows, heads_here, DH)

time: 832 us -> 787 us (0.946)
  waiting for transfers between devices: 610 us -> 547 us
  local copies, waits for them, and re-layouts: 74.6 us -> 87.8 us
    ppermute x0 -> x2, waiting for transfers between devices: none -> 85.2 us  [doubled_up(): lax.ppermute(line, axis, [(d, (d - have) % ways) for d in range(ways)])]
    all_gather x1, waiting for transfers between devices: 54.7 us -> 0.01 us  [shards(): lax.all_gather(kv_mine, 'seq', axis=0, tiled=True)]
    all_gather x1, waiting for transfers between devices: 218 us -> 171 us  [shards(): lax.all_gather(query_weight, 'seq', axis=0, tiled=True)]
    all_gather x1 -> x0, waiting for transfers between devices: 46 us -> none  [shards(): lax.all_gather(normed, 'heads', axis=1, tiled=True)]
  transfers between devices with their start and end apart: 9 -> 10, of which waited for: 9 -> 9; matrix products, arithmetic and copies ran while one was open for 2% -> 5% of each run, Pallas kernels for 0% -> 0%
where the time goes in v1:
time: 787 us; the launch traced here: 783 us
  waiting for transfers between devices  547 us (70%)
  local copies, waits for them, and re-layouts  87.8 us (11%)
  matrix products  73.1 us (9%)
  other arithmetic  28.8 us (4%)
  blocking collectives  19.5 us (2%)
  between operations  14.6 us (2%)
  starting transfers between devices  11.6 us (1%)
    all_gather x1, waiting for transfers between devices, shards(): lax.all_gather(out_weight, 'seq', axis=1, tiled=True)  212 us
    all_gather x1, waiting for transfers between devices, shards(): lax.all_gather(query_weight, 'seq', axis=0, tiled=True)  171 us
    ppermute x2, waiting for transfers between devices, doubled_up(): lax.ppermute(line, axis, [(d, (d - have) % ways) for d in range(ways)])  85.2 us
    reduce_scatter x1, waiting for transfers between devices, shards(): lax.psum_scatter(branch.astype(jnp.bfloat16), 'heads', scatter_dimension=...  54.6 us
    dynamic_update_slice x4, local copies, waits for them, and re-layouts, shards(): local_state, local_out = lax.scan(lightning_block, start_state, inputs)  50.6 us
    dot_general x1, matrix products, shards(): jnp.dot(doubled_up(normed, 'heads', 1), projection, preferred_element_typ...  16 us
  transfers between devices with their start and end apart: 10, of which 9 were waited for; matrix products, arithmetic and copies ran while one was open for 5% of the time, Pallas kernels for 0%

profile of v1, /device:TPU:0, one launch (start us, length us, event | category | flops | bytes accessed | tf_op | source)
XLA Modules:
  0.0 783.1 jit_solution(4846934846582647769)
XLA Ops:
  7.3 2.6 copy.92
  9.9 2.5 copy.93
  13.6 82.6 %while.34 = (s32[]{:T(128)}, f32[8,128,128]{2,1,0:T(8,128)}, f32[2,256,8,128]{1,0,3,2:T(2,128)}, f32[2,256,8]{1,2,0:T(8,128)S(1)}, bf16[2,256,8,128]{3,2,1,0:T(8...) while((s32[]{:T(128)}, f32[8,128,128]{2,1,0:T(8,128)}, ...), condition=%wide.region_3.4_spmd.clone, body=%wide.region_0.3_spmd.clone.sunk | while | flops 1078530048 | bytes 15450984 | solution.py:71
  14.5 2.3 constant_dynamic-slice_fusion.7
  16.8 3.4 convolution_bitcast_fusion.2
  20.2 1.9 constant_dynamic-slice_fusion.6
  22.2 3.7 fusion.87
  25.9 3.3 copy.136
  29.2 22.0 %dynamic_update_slice.6 = f32[2,256,8,128]{1,0,3,2:T(2,128)} dynamic-update-slice(f32[2,256,8,128]{1,0,3,2:T(2,128)} %get-tuple-element.454, f32[1,256,8,128]{1,0,3,2:T(1,128)} %copy.136, s32[]{:T(128)} %get-tuple-element.452, s32[]{:T(128)} %constant.126.clone.1..sunk, s32[]{:T(128)} %constant.126.clone.1..sunk, s32[]{:T(128)} %constant.126.clone.1..sunk) | dynamic-update-slice | bytes 2097156 | tf_op jit(solution)/shard_map/while/body/jit(dynamic_update_index_in_dim)/dynamic_update_slice | solution.py:71
  51.4 3.4 convolution_add_fusion.2
  55.6 2.3 constant_dynamic-slice_fusion.7
  57.9 3.6 convolution_bitcast_fusion.2
  63.5 3.7 fusion.87
  67.2 3.3 copy.136
  70.5 22.0 %dynamic_update_slice.6 = f32[2,256,8,128]{1,0,3,2:T(2,128)} dynamic-update-slice(f32[2,256,8,128]{1,0,3,2:T(2,128)} %get-tuple-element.454, f32[1,256,8,128]{1,0,3,2:T(1,128)} %copy.136, s32[]{:T(128)} %get-tuple-element.452, s32[]{:T(128)} %constant.126.clone.1..sunk, s32[]{:T(128)} %constant.126.clone.1..sunk, s32[]{:T(128)} %constant.126.clone.1..sunk) | dynamic-update-slice | bytes 2097156 | tf_op jit(solution)/shard_map/while/body/jit(dynamic_update_index_in_dim)/dynamic_update_slice | solution.py:71
  92.7 3.5 convolution_add_fusion.2
  100.5 13.7 %all-reduce = bf16[32]{0:T(256)(128)(2,1)S(1)} all-reduce(bf16[32]{0:T(256)(128)(2,1)S(1)} %dynamic-update-slice), channel_id=2, replica_groups=mesh['groups'=2,'heads'=4,'seq'=4] {'seq'}, use_global_device_ids=true, to_apply=%add | all-reduce | flops 32 | bytes 128
  114.4 3.9 reshape.219
  119.9 9.1 %all-gather.12.cloned.1.call-done = bf16[32,128,128]{2,1,0:T(8,128)(2,1)} async-done(((bf16[8,128,128]{2,1,0:T(8,128)(2,1)}), bf16[32,128,128]{2,1,0:T(8,128)(2,1)}) %all-gather.12.cloned.1.call-update) | async-done | bytes 1048592 | tf_op jit(solution)/shard_map/all_gather | solution.py:78
  130.5 4.7 multiply_reduce_fusion.2
  136.5 211.6 %all-gather.8.cloned.1.call-done = bf16[1024,6144]{1,0:T(8,128)(2,1)} async-done(((bf16[1024,1536]{1,0:T(8,128)(2,1)}), bf16[1024,6144]{1,0:T(8,128)(2,1)}) %all-gather.8.cloned.1.call-update) | async-done | bytes 12582928 | tf_op jit(solution)/shard_map/all_gather | solution.py:103
  348.1 11.8 %convolution_convert_fusion = bf16[512,6144]{1,0:T(8,128)(2,1)} fusion(bf16[512,1024]{0,1:T(8,128)(2,1)} %bitcast.180, bf16[1024,6144]{1,0:T(8,128)(2,1)} %all-gather.8.cloned.1.call-done), kind=kOutput, calls=%fused_computation.60 | convolution fusion | flops 6445596672 | bytes 19922944 | tf_op jit(solution)/shard_map/dot_general | solution.py:101
  361.6 54.6 %reduce-scatter.2.cloned.1.call-done = bf16[512,1536]{1,0:T(8,128)(2,1)} async-done(((bf16[512,6144]{1,0:T(8,128)(2,1)}), bf16[512,1536]{1,0:T(8,128)(2,1)}) %reduce-scatter.2.cloned.1.call-update) | async-done | bytes 1572880 | tf_op jit(solution)/shard_map/reduce_scatter | solution.py:113
  416.2 3.1 multiply_reduce_fusion
  419.3 5.7 psum.7
  425.1 3.3 constant_dynamic-update-slice_fusion.5
  428.4 17.9 %collective-permute-done.1 = bf16[512,1536]{1,0:T(8,128)(2,1)S(1)} collective-permute-done((bf16[512,1536]{1,0:T(8,128)(2,1)S(1)}, bf16[512,1536]{1,0:T(8,128)(2,1)S(1)}, u32[]{:S(2)}, u32[]{:S(2)}) %collective-permute-start.1) | collective-permute-done | bytes 1572896 | tf_op jit(solution)/shard_map/ppermute | solution.py:18
  446.3 2.1 pad_maximum_fusion
  451.4 67.3 %collective-permute-done.2 = bf16[512,3072]{1,0:T(8,128)(2,1)} collective-permute-done((bf16[512,3072]{1,0:T(8,128)(2,1)}, bf16[512,3072]{1,0:T(8,128)(2,1)}, u32[]{:S(2)}, u32[]{:S(2)}) %collective-permute-start.2) | collective-permute-done | bytes 3145760 | tf_op jit(solution)/shard_map/ppermute | solution.py:18
  518.6 3.8 constant_dynamic-update-slice_fusion.3
  525.0 3.8 constant_dynamic-update-slice_fusion
  528.9 171.1 %all-gather.10.cloned.1.call-done = bf16[6144,1024]{1,0:T(8,128)(2,1)} async-done(((bf16[1536,1024]{1,0:T(8,128)(2,1)}), bf16[6144,1024]{1,0:T(8,128)(2,1)}) %all-gather.10.cloned.1.call-update) | async-done | bytes 12582928 | tf_op jit(solution)/shard_map/all_gather | solution.py:109
  700.0 16.0 %fusion.44 = bf16[512,1280]{1,0:T(8,128)(2,1)S(1)} fusion(bf16[6144,256]{1,0:T(8,128)(2,1)} %bitcast.187, bf16[6144,1024]{1,0:T(8,128)(2,1)} %all-gather.10.cloned.1.call-done, bf16[512,12288]{1,0:T(8,128)(2,1)} %constant_dynamic-update-slice_fusion, s32[]{:T(128)S(6)} %select_n.65), kind=kOutput, calls=%fused_computation.73 | convolution fusion | flops 8085176320 | bytes 23330820 | tf_op jit(solution)/shard_map/dot_general | solution.py:124
  717.7 2.3 fusion.40
  720.0 3.9 fusion.52
  724.0 49.8 %while.33 = (s32[]{:T(128)}, bf16[512,256]{1,0:T(8,128)(2,1)S(1)}, f32[8,512]{1,0:T(8,128)S(1)}, f32[8,512]{1,0:T(8,128)S(1)}, f32[8,512,128]{2,1,0:T(8,128)}, /...) while((s32[]{:T(128)}, bf16[512,256]{1,0:T(8,128)(2,1)S(1)}, ...), condition=%wide.region_18.19_spmd.clone, body=%wide.region_15.18_spmd.clone.sunk | while | flops 1102587904 | bytes 50341096 | solution.py:170
  725.6 5.7 collective-permute-done
  732.8 2.0 fusion.82
  734.9 3.1 multiply_add_fusion.5
  739.4 4.4 collective-permute-start
  744.0 4.8 collective-permute-done
  750.4 2.0 fusion.82
  752.5 3.1 multiply_add_fusion.5
  757.0 4.4 collective-permute-start
  761.7 3.9 collective-permute-done
  767.1 2.0 fusion.82
  769.3 3.1 multiply_add_fusion.5
  773.7 2.9 copy_bitcast_fusion.11
  (122 shorter events, 33.4 us)
Async XLA Ops:
  7.2 352.9 %copy-start = (bf16[4,1536,256]{2,1,0:T(8,128)(2,1)S(1)}, bf16[4,1536,256]{2,1,0:T(8,128)(2,1)}, u32[]{:S(2)}) copy-start(bf16[4,1536,256]{2,1,0:T(8,128)(2,1)} %param.21) | copy-start | bytes 9437188
  7.2 121.8 %all-gather.12.cloned.1.call-start = ((), (), s32[]{:S(2)}) async-start(), calls=%async_computation.4 | async-start | bytes 1310720 | tf_op jit(solution)/shard_map/all_gather | solution.py:78
  7.2 5.1 copy-start.3
  7.3 6.4 copy-start.6
  96.2 2.8 copy-start.8
  98.1 250.1 %all-gather.8.cloned.1.call-start = ((), (), s32[]{:S(2)}) async-start(), calls=%async_computation.1 | async-start | bytes 15728640 | tf_op jit(solution)/shard_map/all_gather | solution.py:103
  98.8 317.4 %reduce-scatter.2.cloned.1.call-start = ((), (), s32[]{:S(2)}) async-start(), calls=%async_computation.2 | async-start | bytes 7864320 | tf_op jit(solution)/shard_map/reduce_scatter | solution.py:113
  360.0 1.6 copy-start.7
  360.0 168.9 %all-gather.14.cloned.1.call-start = ((), (), s32[]{:S(2)}) async-start(), calls=%async_computation.5 | async-start | bytes 3932160 | tf_op jit(solution)/shard_map/all_gather | solution.py:110
  361.0 55.2 %copy-start.2 = (bf16[512,1536]{1,0:T(8,128)(2,1)S(1)}, bf16[512,1536]{1,0:T(8,128)(2,1)}, u32[]{:S(2)}) copy-start(bf16[512,1536]{1,0:T(8,128)(2,1)} %param.17) | copy-start | bytes 4718596
  361.0 338.9 %all-gather.10.cloned.1.call-start = ((), (), s32[]{:S(2)}) async-start(), calls=%async_computation.3 | async-start | bytes 15728640 | tf_op jit(solution)/shard_map/all_gather | solution.py:109
  428.4 17.9 %collective-permute-start.1 = (bf16[512,1536]{1,0:T(8,128)(2,1)S(1)}, bf16[512,1536]{1,0:T(8,128)(2,1)S(1)}, u32[]{:S(2)}, u32[]{:S(2)}) collective-permute-start(bf16[512,1536]{1,0:T(8,128)(2,1)S(1)} %get-tuple-element.315), channel_id=1, source_target_pairs={{0,12},{4,0},{8,4},{12,8},{1,13},{5,1},{9,5},{13,9},{2,14},{6,2},{... | collective-permute-start | bytes 4718600 | tf_op jit(solution)/shard_map/ppermute | solution.py:18
  448.4 70.2 %collective-permute-start.2 = (bf16[512,3072]{1,0:T(8,128)(2,1)}, bf16[512,3072]{1,0:T(8,128)(2,1)}, u32[]{:S(2)}, u32[]{:S(2)}) collective-permute-start(bf16[512,3072]{1,0:T(8,128)(2,1)} %pad_maximum_fusion), channel_id=1, source_target_pairs={{0,8},{4,12},{8,0},{12,4},{1,9},{5,13},{9,1},{13,5},{2,10},{6,14},... | collective-permute-start | bytes 9437192 | tf_op jit(solution)/shard_map/ppermute | solution.py:18
  724.0 7.2 collective-permute-start
  732.8 2.1 copy-start.4
  738.0 1.4 copy-start.5
  739.4 9.5 %collective-permute-start = (bf16[512,256]{1,0:T(8,128)(2,1)S(1)}, bf16[512,256]{1,0:T(8,128)(2,1)S(1)}, u32[]{:S(2)}, u32[]{:S(2)}) collective-permute-start(bf16[512,256]{1,0:T(8,128)(2,1)S(1)} %get-tuple-element.483), channel_id=1, source_target_pairs={{0,1},{1,2},{2,3},{4,5},{5,6},{6,7},{8,9},{9,10},{10,11},{12,13},{... | collective-permute-start | bytes 786440 | tf_op jit(solution)/shard_map/while/body/eval_jaxpr/ppermute | solution.py:28
  750.4 2.1 copy-start.4
  755.6 1.4 copy-start.5
  757.0 8.6 %collective-permute-start = (bf16[512,256]{1,0:T(8,128)(2,1)S(1)}, bf16[512,256]{1,0:T(8,128)(2,1)S(1)}, u32[]{:S(2)}, u32[]{:S(2)}) collective-permute-start(bf16[512,256]{1,0:T(8,128)(2,1)S(1)} %get-tuple-element.483), channel_id=1, source_target_pairs={{0,1},{1,2},{2,3},{4,5},{5,6},{6,7},{8,9},{9,10},{10,11},{12,13},{... | collective-permute-start | bytes 786440 | tf_op jit(solution)/shard_map/while/body/eval_jaxpr/ppermute | solution.py:28
  767.1 2.1 copy-start.4
  772.4 1.4 copy-start.5
  773.7 2.9 copy-start.1
Sparse Core Ops, SparseCore 0:
  98.2 30.7 all-gather.11
  130.5 217.5 all-gather.7
  360.1 56.0 reduce-scatter.1
  418.2 63.4 all-gather.13
  483.1 216.8 all-gather.9
